TPU v7x, 512 devices: a whole 4x4x16 slice. The times are simulated.
512 devices in a mesh: patch: 16 (over y, x_hi, core), map: 32 (over x_lo, z).
Axes of the slice: x: 4 (x_hi: 2, x_lo: 2; x = x_hi * 2 + x_lo), y: 4, z: 16, core: 2. Of those that a mesh axis runs over, the one named last changes fastest.
Arguments:
- maps: bfloat16 [64, 32, 24576], P('map', None, 'patch'), may hold values from -6 to 6
- cotangent: bfloat16 [64, 32, 24576], P('map', None, 'patch'), may hold values from -6 to 6
- tiles: bfloat16 [96, 3, 256, 256], P('patch'), may hold values from -0.21875 to 0.21875
- columns: int32 [96, 3], P('patch'), may hold values from 0 to 95, as said below
- filters: bfloat16 [3, 32, 32], replicated, may hold values from -0.625 to 0.625
Outputs:
- output: bfloat16 [64, 32, 24576], P('map', None, 'patch')
- input_grad: bfloat16 [64, 32, 24576], P('map', None, 'patch')
- filter_grad: float32 [3, 32, 32], replicated
Inputs may be any that keep to these rules, and one draw needn't show every extreme that they name: `columns`: slot 0 of block row b names block b itself, slot 1 a block 1 to 2 before it and slot 2 a block 1 to 2 after it, counted cyclically over the 96 blocks; block row 0 reads exactly 2 blocks away on both sides.
All inputs are finite; a program needn't handle non-finite values.
Results may differ from a plain program's by a relative error of at most 0.0054.
Values may be sent and summed in bfloat16 or wider, within the bound.
No kernel may reach another device: no remote copies, remote signals or barrier semaphores. Data moves between devices by JAX's collectives and lax.ppermute only.
A program may use at most 64 MiB of HBM per device.

v0:
```python
import math
import jax
import jax.numpy as jnp
from jax import lax
from jax.sharding import PartitionSpec as P

REACH = 2


def extended_2(cells, sides, width):
    for axis, dim in sides:
        count = lax.axis_size(axis)
        head = lax.slice_in_dim(cells, 0, width, axis=dim)
        tail = lax.slice_in_dim(cells, cells.shape[dim] - width, cells.shape[dim], axis=dim)
        cells = jnp.concatenate(
            [
                lax.ppermute(tail, axis, [(i, (i + 1) % count) for i in range(count)]),
                cells,
                lax.ppermute(head, axis, [((i + 1) % count, i) for i in range(count)]),
            ],
            axis=dim,
        )
    return cells


def offset_sums(grad_blocks, tile_set, offset_mask):
    contrib = jnp.einsum(
        "nui,ujiq->nujq", grad_blocks, tile_set, preferred_element_type=jnp.float32
    )
    return jnp.einsum(
        "uje,nujq->nueq", offset_mask.astype(jnp.float32), contrib, precision=lax.Precision.HIGHEST
    )


def per_device(maps, cotangent, tiles, columns, filters):
    map_count = maps.shape[0]
    chan_count = maps.shape[1]
    pix_count = maps.shape[2]
    block_count = tiles.shape[0]
    block_size = tiles.shape[2]
    reach_blocks = REACH
    spread = 2 * reach_blocks + 1
    row_count = map_count * chan_count
    rim_cells = reach_blocks * block_size
    patch_count = lax.axis_size("patch")
    total_blocks = block_count * patch_count
    first_block = lax.axis_index("patch") * block_count
    row_ids = first_block + jnp.arange(block_count, dtype=jnp.int32)
    offset_ids = jnp.arange(spread, dtype=jnp.int32)
    own_offset = (columns - row_ids[:, None] + reach_blocks) % total_blocks
    own_mask = own_offset[:, :, None] == offset_ids[None, None, :]

    def forward_apply(field):
        extended = extended_2(field, (("patch", 2),), rim_cells)
        ext_blocks = extended.reshape(row_count, block_count + 2 * reach_blocks, block_size)
        shifted = jnp.stack(
            [ext_blocks[:, offset : offset + block_count] for offset in range(spread)], axis=2
        )
        picked = jnp.einsum(
            "rje,nreq->nrjq",
            own_mask.astype(jnp.bfloat16),
            shifted,
            preferred_element_type=jnp.bfloat16,
        )
        result = jnp.einsum("nrjq,rjiq->nri", picked, tiles, preferred_element_type=jnp.float32)
        return result.reshape(map_count, chan_count, pix_count)

    def adjoint_apply(grads):
        by_offset = offset_sums(grads.reshape(row_count, block_count, block_size), tiles, own_mask)
        window = jnp.pad(by_offset[:, :, 0], ((0, 0), (0, spread - 1), (0, 0)))
        for offset in range(1, spread):
            window = window + jnp.pad(
                by_offset[:, :, offset], ((0, 0), (offset, spread - 1 - offset), (0, 0))
            )
        own_part = window[:, reach_blocks : reach_blocks + block_count]
        outgoing = jnp.concatenate(
            [window[:, :reach_blocks], window[:, reach_blocks + block_count :]], axis=1
        )
        outgoing = outgoing.reshape(map_count, chan_count, 2 * rim_cells)
        incoming = extended_2(outgoing, (("patch", 2),), rim_cells)
        from_left = incoming[:, :, :rim_cells].reshape(row_count, reach_blocks, block_size)
        from_right = incoming[:, :, incoming.shape[2] - rim_cells :].reshape(
            row_count, reach_blocks, block_size
        )
        own_part = own_part.at[:, :reach_blocks].add(from_left)
        own_part = own_part.at[:, block_count - reach_blocks :].add(from_right)
        return own_part.reshape(map_count, chan_count, pix_count)

    x_one = forward_apply(maps).astype(jnp.bfloat16)
    x_two = (2.0 * forward_apply(x_one) - maps.astype(jnp.float32)).astype(jnp.bfloat16)
    terms = jnp.stack([maps, x_one, x_two])
    output = jnp.einsum("kco,kmcp->mop", filters, terms, preferred_element_type=jnp.float32).astype(
        jnp.bfloat16
    )
    grads = jnp.einsum("kco,mop->kmcp", filters, cotangent, preferred_element_type=jnp.float32)
    grad_two = grads[2].astype(jnp.bfloat16)
    update = (grads[1] + 2.0 * adjoint_apply(grad_two)).astype(jnp.bfloat16)
    input_grad = (grads[0] - grad_two.astype(jnp.float32) + adjoint_apply(update)).astype(
        jnp.bfloat16
    )
    scale = 1.0 / math.sqrt(map_count * lax.axis_size("map") * pix_count * patch_count)
    local_grad = jnp.einsum("kmcp,mop->kco", terms, cotangent, preferred_element_type=jnp.float32)
    filter_grad = lax.psum(local_grad, ("patch", "map")) * scale
    return (output, input_grad, filter_grad)


def solution(mesh):
    placed = (
        P("map", None, "patch"),
        P("map", None, "patch"),
        P("patch", None, None, None),
        P("patch", None),
        P(),
    )
    return jax.shard_map(
        per_device,
        mesh=mesh,
        in_specs=placed,
        out_specs=(P("map", None, "patch"), P("map", None, "patch"), P()),
        check_vma=False,
    )
```

profile of v0, /device:TPU:1, one launch (start us, length us, event | category | flops | bytes accessed | tf_op | source)
XLA Modules:
  0.0 221.6 jit_solution(9846326644404595408)
XLA Ops:
  1.6 1.2 convolution_bitcast_fusion
  2.8 1.0 copy-done.15
  4.6 2.3 %convolution_bitcast_fusion.3 = f32[64,6,5,256]{3,2,0,1:T(8,128)S(1)} fusion(f32[6,64,3,256]{3,1,2,0:T(8,128)S(1)} %fusion.38, s32[6,3]{1,0:T(8,128)S(1)} %copy.21), kind=kOutput, calls=%fused_computation.5 | convolution fusion | flops 17694810 | bytes 3145800 | tf_op jit(solution)/shard_map/uje,nujq->nueq/dot_general | solution.py:30
  6.9 1.8 fusion.56
  10.8 1.8 reshape.181
  12.6 1.8 fusion.58
  14.4 6.0 %collective-permute-start.4 = (f32[2,32,512]{2,1,0:T(8,128)}, f32[2,32,512]{2,1,0:T(8,128)}, u32[]{:S(2)}, u32[]{:S(2)}) collective-permute-start(f32[2,32,512]{2,1,0:T(8,128)} %get-tuple-element.68), channel_id=1, source_target_pairs={{0,32},{32,64},{64,96},{96,128},{128,160},{160,192},{192,224},{224... | collective-permute-start | bytes 393224 | tf_op jit(solution)/shard_map/ppermute | solution.py:17
  20.4 4.7 %collective-permute-start.5 = (f32[2,32,512]{2,1,0:T(8,128)}, f32[2,32,512]{2,1,0:T(8,128)}, u32[]{:S(2)}, u32[]{:S(2)}) collective-permute-start(f32[2,32,512]{2,1,0:T(8,128)} %get-tuple-element.67), channel_id=1, source_target_pairs={{32,0},{64,32},{96,64},{128,96},{160,128},{192,160},{224,192},{256... | collective-permute-start | bytes 393224 | tf_op jit(solution)/shard_map/ppermute | solution.py:19
  25.1 1.5 fusion.60
  26.6 2.4 %collective-permute-start = (bf16[2,32,512]{2,1,0:T(8,128)(2,1)}, bf16[2,32,512]{2,1,0:T(8,128)(2,1)}, u32[]{:S(2)}, u32[]{:S(2)}) collective-permute-start(bf16[2,32,512]{2,1,0:T(8,128)(2,1)} %get-tuple-element.71), channel_id=1, source_target_pairs={{0,32},{32,64},{64,96},{96,128},{128,160},{160,192},{192,224},{224... | collective-permute-start | bytes 196616 | tf_op jit(solution)/shard_map/ppermute | solution.py:17
  29.0 6.8 %collective-permute-start.1 = (bf16[2,32,512]{2,1,0:T(8,128)(2,1)}, bf16[2,32,512]{2,1,0:T(8,128)(2,1)}, u32[]{:S(2)}, u32[]{:S(2)}) collective-permute-start(bf16[2,32,512]{2,1,0:T(8,128)(2,1)} %get-tuple-element.72), channel_id=1, source_target_pairs={{32,0},{64,32},{96,64},{128,96},{160,128},{192,160},{224,192},{256... | collective-permute-start | bytes 196616 | tf_op jit(solution)/shard_map/ppermute | solution.py:19
  35.8 1.8 slice.264
  38.5 1.9 squeeze.35
  40.5 1.6 pad_maximum_fusion.1
  42.1 1.2 reshape.179
  43.6 1.3 fusion.8
  46.6 1.9 convert_element_type.73
  48.4 1.9 convert_element_type.72
  50.3 1.5 fusion.59
  51.8 1.9 collective-permute-start.2
  53.7 7.4 %collective-permute-start.3 = (bf16[2,32,512]{2,1,0:T(8,128)(2,1)}, bf16[2,32,512]{2,1,0:T(8,128)(2,1)}, u32[]{:S(2)}, u32[]{:S(2)}) collective-permute-start(bf16[2,32,512]{2,1,0:T(8,128)(2,1)} %get-tuple-element.70), channel_id=1, source_target_pairs={{32,0},{64,32},{96,64},{128,96},{160,128},{192,160},{224,192},{256... | collective-permute-start | bytes 196616 | tf_op jit(solution)/shard_map/ppermute | solution.py:19
  61.2 1.6 reshape.182
  62.8 1.7 fusion.44
  64.5 1.0 reshape.183
  65.5 1.6 fusion.43
  67.1 1.6 fusion.34
  68.7 2.3 %convolution_bitcast_fusion.2 = f32[64,6,5,256]{3,2,0,1:T(8,128)S(1)} fusion(f32[6,64,3,256]{3,1,2,0:T(8,128)S(1)} %fusion.34, s32[6,3]{1,0:T(8,128)S(1)} %copy.21), kind=kOutput, calls=%fused_computation.4 | convolution fusion | flops 17694810 | bytes 3145800 | tf_op jit(solution)/shard_map/uje,nujq->nueq/dot_general | solution.py:30
  71.0 1.8 fusion.55
  73.1 1.2 pad_add_fusion
  75.3 1.6 pad_maximum_fusion.2
  76.9 1.2 reshape.180
  78.4 1.3 fusion.6
  81.7 1.1 fusion.32
  82.8 2.0 convolution_bitcast_fusion.6
  86.7 1.8 reshape.184
  88.4 1.7 fusion.57
  90.1 1.9 collective-permute-start.6
  92.0 1.8 slice.279
  93.8 7.2 %collective-permute-start.7 = (f32[2,32,512]{2,1,0:T(8,128)}, f32[2,32,512]{2,1,0:T(8,128)}, u32[]{:S(2)}, u32[]{:S(2)}) collective-permute-start(f32[2,32,512]{2,1,0:T(8,128)} %get-tuple-element.65), channel_id=1, source_target_pairs={{32,0},{64,32},{96,64},{128,96},{160,128},{192,160},{224,192},{256... | collective-permute-start | bytes 393224 | tf_op jit(solution)/shard_map/ppermute | solution.py:19
  101.0 106.8 %psum.7 = f32[3,32,32]{2,1,0:T(8,128)} all-reduce(f32[3,32,32]{2,1,0:T(8,128)} %convolution_bitcast_fusion.6), channel_id=1, replica_groups=mesh['patch'=16,'map'=32] {'patch','map'}, use_global_device_ids=true, to_apply=%region_0.1 | all-reduce | flops 3072 | bytes 24576 | tf_op jit(solution)/shard_map/psum | solution.py:103
  207.8 1.4 broadcast_multiply_fusion
  209.2 1.6 reshape.185
  210.9 1.7 fusion.42
  212.5 1.7 reshape.186
  214.3 1.6 fusion.41
  215.9 2.0 copy.42
  218.0 1.9 reshape.187
  219.9 1.7 fusion.20
  (93 shorter events, 11.9 us)
Async XLA Ops:
  0.6 3.5 %copy-start = (bf16[6,3,256,256]{3,2,1,0:T(8,128)(2,1)S(1)}, bf16[6,3,256,256]{3,2,1,0:T(8,128)(2,1)}, u32[]{:S(2)}) copy-start(bf16[6,3,256,256]{3,2,1,0:T(8,128)(2,1)} %param.15) | copy-start | bytes 7077892
  2.8 1.0 copy-start.15
  8.9 28.7 %copy-start.7 = (f32[64,6,256]{2,0,1:T(8,128)}, f32[64,6,256]{2,0,1:T(8,128)S(1)}, u32[]{:S(2)}) copy-start(f32[64,6,256]{2,0,1:T(8,128)S(1)} %get-tuple-element.73) | copy-start | bytes 1179652
  8.9 28.7 %copy-start.9 = (f32[64,6,256]{2,0,1:T(8,128)}, f32[64,6,256]{2,0,1:T(8,128)S(1)}, u32[]{:S(2)}) copy-start(f32[64,6,256]{2,0,1:T(8,128)S(1)} %get-tuple-element.74) | copy-start | bytes 1179652
  9.0 0.8 copy-start.11
  9.0 1.0 copy-start.13
  12.6 25.0 %copy-start.12 = (f32[64,6,256]{2,0,1:T(8,128)S(1)}, f32[64,6,256]{2,0,1:T(8,128)}, u32[]{:S(2)}) copy-start(f32[64,6,256]{2,0,1:T(8,128)} %copy-done.11) | copy-start | bytes 1179652
  12.6 25.0 %copy-start.14 = (f32[64,6,256]{2,0,1:T(8,128)S(1)}, f32[64,6,256]{2,0,1:T(8,128)}, u32[]{:S(2)}) copy-start(f32[64,6,256]{2,0,1:T(8,128)} %copy-done.13) | copy-start | bytes 1179652
  14.4 46.8 %collective-permute-start.4 = (f32[2,32,512]{2,1,0:T(8,128)}, f32[2,32,512]{2,1,0:T(8,128)}, u32[]{:S(2)}, u32[]{:S(2)}) collective-permute-start(f32[2,32,512]{2,1,0:T(8,128)} %get-tuple-element.68), channel_id=1, source_target_pairs={{0,32},{32,64},{64,96},{96,128},{128,160},{160,192},{192,224},{224... | collective-permute-start | bytes 393224 | tf_op jit(solution)/shard_map/ppermute | solution.py:17
  20.4 44.1 %collective-permute-start.5 = (f32[2,32,512]{2,1,0:T(8,128)}, f32[2,32,512]{2,1,0:T(8,128)}, u32[]{:S(2)}, u32[]{:S(2)}) collective-permute-start(f32[2,32,512]{2,1,0:T(8,128)} %get-tuple-element.67), channel_id=1, source_target_pairs={{32,0},{64,32},{96,64},{128,96},{160,128},{192,160},{224,192},{256... | collective-permute-start | bytes 393224 | tf_op jit(solution)/shard_map/ppermute | solution.py:19
  26.6 13.8 %collective-permute-start = (bf16[2,32,512]{2,1,0:T(8,128)(2,1)}, bf16[2,32,512]{2,1,0:T(8,128)(2,1)}, u32[]{:S(2)}, u32[]{:S(2)}) collective-permute-start(bf16[2,32,512]{2,1,0:T(8,128)(2,1)} %get-tuple-element.71), channel_id=1, source_target_pairs={{0,32},{32,64},{64,96},{96,128},{128,160},{160,192},{192,224},{224... | collective-permute-start | bytes 196616 | tf_op jit(solution)/shard_map/ppermute | solution.py:17
  29.0 11.4 %collective-permute-start.1 = (bf16[2,32,512]{2,1,0:T(8,128)(2,1)}, bf16[2,32,512]{2,1,0:T(8,128)(2,1)}, u32[]{:S(2)}, u32[]{:S(2)}) collective-permute-start(bf16[2,32,512]{2,1,0:T(8,128)(2,1)} %get-tuple-element.72), channel_id=1, source_target_pairs={{32,0},{64,32},{96,64},{128,96},{160,128},{192,160},{224,192},{256... | collective-permute-start | bytes 196616 | tf_op jit(solution)/shard_map/ppermute | solution.py:19
  37.7 2.7 %copy-start.18 = (bf16[2,32,1536]{2,1,0:T(8,128)(2,1)S(1)}, bf16[2,32,1536]{2,1,0:T(8,128)(2,1)}, u32[]{:S(2)}) copy-start(bf16[2,32,1536]{2,1,0:T(8,128)(2,1)} %param.13) | copy-start | bytes 589828
  45.7 17.1 %copy-start.8 = (f32[64,6,256]{2,0,1:T(8,128)S(1)}, f32[64,6,256]{2,0,1:T(8,128)}, u32[]{:S(2)}) copy-start(f32[64,6,256]{2,0,1:T(8,128)} %copy-done.7) | copy-start | bytes 1179652
  45.7 17.1 %copy-start.10 = (f32[64,6,256]{2,0,1:T(8,128)S(1)}, f32[64,6,256]{2,0,1:T(8,128)}, u32[]{:S(2)}) copy-start(f32[64,6,256]{2,0,1:T(8,128)} %copy-done.9) | copy-start | bytes 1179652
  51.8 23.2 %collective-permute-start.2 = (bf16[2,32,512]{2,1,0:T(8,128)(2,1)}, bf16[2,32,512]{2,1,0:T(8,128)(2,1)}, u32[]{:S(2)}, u32[]{:S(2)}) collective-permute-start(bf16[2,32,512]{2,1,0:T(8,128)(2,1)} %get-tuple-element.69), channel_id=1, source_target_pairs={{0,32},{32,64},{64,96},{96,128},{128,160},{160,192},{192,224},{224... | collective-permute-start | bytes 196616 | tf_op jit(solution)/shard_map/ppermute | solution.py:17
  53.7 21.3 %collective-permute-start.3 = (bf16[2,32,512]{2,1,0:T(8,128)(2,1)}, bf16[2,32,512]{2,1,0:T(8,128)(2,1)}, u32[]{:S(2)}, u32[]{:S(2)}) collective-permute-start(bf16[2,32,512]{2,1,0:T(8,128)(2,1)} %get-tuple-element.70), channel_id=1, source_target_pairs={{32,0},{64,32},{96,64},{128,96},{160,128},{192,160},{224,192},{256... | collective-permute-start | bytes 196616 | tf_op jit(solution)/shard_map/ppermute | solution.py:19
  72.9 1.3 copy-start.1
  73.0 1.3 copy-start.3
  73.0 1.3 copy-start.5
  73.0 1.2 copy-start.6
  74.3 1.0 copy-start.17
  80.6 1.1 copy-start.19
  81.7 3.1 %copy-start.22 = (bf16[1,2,32,1536]{3,2,1,0:T(8,128)(2,1)S(1)}, bf16[1,2,32,1536]{3,2,1,0:T(8,128)(2,1)}, u32[]{:S(2)}) copy-start(bf16[1,2,32,1536]{3,2,1,0:T(8,128)(2,1)} %convert_element_type.72) | copy-start | bytes 589828
  81.7 3.1 %copy-start.23 = (bf16[3,32,32]{2,1,0:T(8,128)(2,1)S(1)}, bf16[3,32,32]{2,1,0:T(8,128)(2,1)}, u32[]{:S(2)}) copy-start(bf16[3,32,32]{2,1,0:T(8,128)(2,1)} %param.17) | copy-start | bytes 18436
  82.8 3.0 %copy-start.20 = (f32[64,2,256]{2,0,1:T(8,128)S(1)}, f32[64,2,256]{2,0,1:T(8,128)}, u32[]{:S(2)}) copy-start(f32[64,2,256]{2,0,1:T(8,128)} %get-tuple-element.61) | copy-start | bytes 393220
  82.8 3.0 %copy-start.21 = (f32[64,2,256]{2,0,1:T(8,128)S(1)}, f32[64,2,256]{2,0,1:T(8,128)}, u32[]{:S(2)}) copy-start(f32[64,2,256]{2,0,1:T(8,128)} %get-tuple-element.62) | copy-start | bytes 393220
  85.8 125.1 %copy-start.2 = (f32[64,6,1,256]{3,0,1,2:T(8,128)S(1)}, f32[64,6,1,256]{3,0,1,2:T(8,128)}, u32[]{:S(2)}) copy-start(f32[64,6,1,256]{3,0,1,2:T(8,128)} %copy-done.1) | copy-start | bytes 1179652
  85.8 125.1 %copy-start.4 = (f32[64,6,1,256]{3,0,1,2:T(8,128)S(1)}, f32[64,6,1,256]{3,0,1,2:T(8,128)}, u32[]{:S(2)}) copy-start(f32[64,6,1,256]{3,0,1,2:T(8,128)} %copy-done.3) | copy-start | bytes 1179652
  90.1 119.1 %collective-permute-start.6 = (f32[2,32,512]{2,1,0:T(8,128)}, f32[2,32,512]{2,1,0:T(8,128)}, u32[]{:S(2)}, u32[]{:S(2)}) collective-permute-start(f32[2,32,512]{2,1,0:T(8,128)} %get-tuple-element.66), channel_id=1, source_target_pairs={{0,32},{32,64},{64,96},{96,128},{128,160},{160,192},{192,224},{224... | collective-permute-start | bytes 393224 | tf_op jit(solution)/shard_map/ppermute | solution.py:17
  93.8 118.8 %collective-permute-start.7 = (f32[2,32,512]{2,1,0:T(8,128)}, f32[2,32,512]{2,1,0:T(8,128)}, u32[]{:S(2)}, u32[]{:S(2)}) collective-permute-start(f32[2,32,512]{2,1,0:T(8,128)} %get-tuple-element.65), channel_id=1, source_target_pairs={{32,0},{64,32},{96,64},{128,96},{160,128},{192,160},{224,192},{256... | collective-permute-start | bytes 393224 | tf_op jit(solution)/shard_map/ppermute | solution.py:19
  212.5 7.3 %copy-start.16 = (f32[3,2,32,1536]{3,2,0,1:T(8,128)S(1)}, f32[3,2,32,1536]{3,2,0,1:T(8,128)}, u32[]{:S(2)}) copy-start(f32[3,2,32,1536]{3,2,0,1:T(8,128)} %copy-done.15) | copy-start | bytes 3538948
where the time goes:
time: 223 us; the launch traced here: 222 us
  blocking collectives  107 us (48%)
  local copies, waits for them, and re-layouts  43.2 us (19%)
  starting transfers between devices  38.4 us (17%)
  other arithmetic  17 us (8%)
  matrix products  15.1 us (7%)
    psum x1, blocking collectives, per_device(): filter_grad = lax.psum(local_grad, ('patch', 'map')) * scale  107 us
    ppermute x4, starting transfers between devices, extended_2(): lax.ppermute(head, axis, [((i + 1) % count, i) for i in range(count)])  26.1 us
    ppermute x4, starting transfers between devices, extended_2(): lax.ppermute(tail, axis, [(i, (i + 1) % count) for i in range(count)])  12.2 us
    another operation x4, local copies, waits for them, and re-layouts  6 us
    dot_general x2, matrix products, offset_sums(): jnp.einsum('uje,nujq->nueq', offset_mask.astype(jnp.float32), contrib, pr...  4.57 us
    convert_element_type x3, local copies, waits for them, and re-layouts, per_device(): x_one = forward_apply(maps).astype(jnp.bfloat16)  4.53 us
  transfers between devices with their start and end apart: 8, of which 0 were waited for; matrix products, arithmetic and copies ran while one was open for 17% of the time, Pallas kernels for 0%

commit v1 on v0

--- a/solution.py
+++ b/solution.py
@@ -100,7 +100,7 @@
     )
     scale = 1.0 / math.sqrt(map_count * lax.axis_size("map") * pix_count * patch_count)
     local_grad = jnp.einsum("kmcp,mop->kco", terms, cotangent, preferred_element_type=jnp.float32)
-    filter_grad = lax.psum(local_grad, ("patch", "map")) * scale
+    filter_grad = lax.psum(lax.psum(local_grad, "map"), "patch") * scale
     return (output, input_grad, filter_grad)
 
 

time: 223 us -> 310 us (1.39); the launches traced: 222 us -> 304 us
  blocking collectives: 107 us -> 189 us
    psum x1 -> x2, blocking collectives: 107 us -> 189 us  [per_device(): filter_grad = lax.psum(lax.psum(local_grad, 'map'), 'patch') * scale]
  transfers between devices with their start and end apart: 8 -> 8, of which waited for: 0 -> 0; matrix products, arithmetic and copies ran while one was open for 17% -> 12% of each run, Pallas kernels for 0% -> 0%
where the time goes in v1:
time: 310 us; the launch traced here: 304 us
  blocking collectives  189 us (61%)
  local copies, waits for them, and re-layouts  43.3 us (14%)
  starting transfers between devices  38.4 us (12%)
  other arithmetic  17 us (5%)
  matrix products  15.1 us (5%)
    psum x2, blocking collectives, per_device(): filter_grad = lax.psum(lax.psum(local_grad, 'map'), 'patch') * scale  189 us
    ppermute x4, starting transfers between devices, extended_2(): lax.ppermute(head, axis, [((i + 1) % count, i) for i in range(count)])  26.1 us
    ppermute x4, starting transfers between devices, extended_2(): lax.ppermute(tail, axis, [(i, (i + 1) % count) for i in range(count)])  12.3 us
  transfers between devices with their start and end apart: 8, of which 0 were waited for; matrix products, arithmetic and copies ran while one was open for 12% of the time, Pallas kernels for 0%

profile of v1, /device:TPU:1, one launch (start us, length us, event | category | flops | bytes accessed | tf_op | source)
XLA Modules:
  0.0 304.0 jit_solution(17010179923313687033)
XLA Ops:
  1.6 1.2 convolution_bitcast_fusion
  2.8 1.0 copy-done.15
  4.6 2.3 convolution_bitcast_fusion.3
  6.9 1.8 fusion.56
  10.8 1.8 reshape.181
  12.6 1.8 fusion.58
  14.4 6.0 %collective-permute-start.4 = (f32[2,32,512]{2,1,0:T(8,128)}, f32[2,32,512]{2,1,0:T(8,128)}, u32[]{:S(2)}, u32[]{:S(2)}) collective-permute-start(f32[2,32,512]{2,1,0:T(8,128)} %get-tuple-element.68), channel_id=1, source_target_pairs={{0,32},{32,64},{64,96},{96,128},{128,160},{160,192},{192,224},{224... | collective-permute-start | bytes 393224 | tf_op jit(solution)/shard_map/ppermute | solution.py:17
  20.4 4.7 %collective-permute-start.5 = (f32[2,32,512]{2,1,0:T(8,128)}, f32[2,32,512]{2,1,0:T(8,128)}, u32[]{:S(2)}, u32[]{:S(2)}) collective-permute-start(f32[2,32,512]{2,1,0:T(8,128)} %get-tuple-element.67), channel_id=1, source_target_pairs={{32,0},{64,32},{96,64},{128,96},{160,128},{192,160},{224,192},{256... | collective-permute-start | bytes 393224 | tf_op jit(solution)/shard_map/ppermute | solution.py:19
  25.1 1.5 fusion.60
  26.6 2.4 collective-permute-start
  29.0 6.8 %collective-permute-start.1 = (bf16[2,32,512]{2,1,0:T(8,128)(2,1)}, bf16[2,32,512]{2,1,0:T(8,128)(2,1)}, u32[]{:S(2)}, u32[]{:S(2)}) collective-permute-start(bf16[2,32,512]{2,1,0:T(8,128)(2,1)} %get-tuple-element.72), channel_id=1, source_target_pairs={{32,0},{64,32},{96,64},{128,96},{160,128},{192,160},{224,192},{256... | collective-permute-start | bytes 196616 | tf_op jit(solution)/shard_map/ppermute | solution.py:19
  35.8 1.8 slice.264
  38.5 1.9 squeeze.35
  40.4 1.6 pad_maximum_fusion.1
  42.1 1.2 reshape.179
  43.6 1.3 fusion.8
  46.6 1.9 convert_element_type.73
  48.4 1.9 convert_element_type.72
  50.3 1.5 fusion.59
  51.8 1.9 collective-permute-start.2
  53.7 7.4 %collective-permute-start.3 = (bf16[2,32,512]{2,1,0:T(8,128)(2,1)}, bf16[2,32,512]{2,1,0:T(8,128)(2,1)}, u32[]{:S(2)}, u32[]{:S(2)}) collective-permute-start(bf16[2,32,512]{2,1,0:T(8,128)(2,1)} %get-tuple-element.70), channel_id=1, source_target_pairs={{32,0},{64,32},{96,64},{128,96},{160,128},{192,160},{224,192},{256... | collective-permute-start | bytes 196616 | tf_op jit(solution)/shard_map/ppermute | solution.py:19
  61.2 1.7 reshape.182
  62.8 1.7 fusion.44
  65.6 1.6 fusion.43
  67.1 1.6 fusion.34
  68.8 2.3 convolution_bitcast_fusion.2
  71.1 1.8 fusion.55
  73.1 1.2 pad_add_fusion
  75.3 1.6 pad_maximum_fusion.2
  76.9 1.2 reshape.180
  78.5 1.3 fusion.6
  81.7 1.1 fusion.32
  82.8 2.0 convolution_bitcast_fusion.6
  86.7 1.9 reshape.184
  88.5 1.7 fusion.57
  90.2 1.9 collective-permute-start.6
  92.1 1.8 slice.279
  93.9 7.2 %collective-permute-start.7 = (f32[2,32,512]{2,1,0:T(8,128)}, f32[2,32,512]{2,1,0:T(8,128)}, u32[]{:S(2)}, u32[]{:S(2)}) collective-permute-start(f32[2,32,512]{2,1,0:T(8,128)} %get-tuple-element.65), channel_id=1, source_target_pairs={{32,0},{64,32},{96,64},{128,96},{160,128},{192,160},{224,192},{256... | collective-permute-start | bytes 393224 | tf_op jit(solution)/shard_map/ppermute | solution.py:19
  101.2 95.6 %psum.14 = f32[3,32,32]{2,1,0:T(8,128)} all-reduce(f32[3,32,32]{2,1,0:T(8,128)} %convolution_bitcast_fusion.6), channel_id=1, replica_groups=mesh['patch'=16,'map'=32] {'map'}, use_global_device_ids=true, to_apply=%region_0.1 | all-reduce | flops 3072 | bytes 24576 | tf_op jit(solution)/shard_map/psum | solution.py:103
  196.8 93.4 %psum.15 = f32[3,32,32]{2,1,0:T(8,128)} all-reduce(f32[3,32,32]{2,1,0:T(8,128)} %psum.14), channel_id=1, replica_groups=mesh['patch'=16,'map'=32] {'patch'}, use_global_device_ids=true, to_apply=%region_1.2 | all-reduce | flops 3072 | bytes 24576 | tf_op jit(solution)/shard_map/psum | solution.py:103
  290.2 1.4 broadcast_multiply_fusion
  291.6 1.7 reshape.185
  293.2 1.7 fusion.42
  294.9 1.7 reshape.186
  296.7 1.6 fusion.41
  298.3 2.0 copy.42
  300.3 1.9 reshape.187
  302.2 1.7 fusion.20
  (94 shorter events, 12.9 us)
Async XLA Ops:
  0.6 3.5 %copy-start = (bf16[6,3,256,256]{3,2,1,0:T(8,128)(2,1)S(1)}, bf16[6,3,256,256]{3,2,1,0:T(8,128)(2,1)}, u32[]{:S(2)}) copy-start(bf16[6,3,256,256]{3,2,1,0:T(8,128)(2,1)} %param.15) | copy-start | bytes 7077892
  2.8 1.0 copy-start.15
  8.8 28.7 %copy-start.7 = (f32[64,6,256]{2,0,1:T(8,128)}, f32[64,6,256]{2,0,1:T(8,128)S(1)}, u32[]{:S(2)}) copy-start(f32[64,6,256]{2,0,1:T(8,128)S(1)} %get-tuple-element.73) | copy-start | bytes 1179652
  8.9 28.7 %copy-start.9 = (f32[64,6,256]{2,0,1:T(8,128)}, f32[64,6,256]{2,0,1:T(8,128)S(1)}, u32[]{:S(2)}) copy-start(f32[64,6,256]{2,0,1:T(8,128)S(1)} %get-tuple-element.74) | copy-start | bytes 1179652
  8.9 0.9 copy-start.11
  8.9 0.9 copy-start.13
  12.6 25.0 %copy-start.12 = (f32[64,6,256]{2,0,1:T(8,128)S(1)}, f32[64,6,256]{2,0,1:T(8,128)}, u32[]{:S(2)}) copy-start(f32[64,6,256]{2,0,1:T(8,128)} %copy-done.11) | copy-start | bytes 1179652
  12.6 25.0 %copy-start.14 = (f32[64,6,256]{2,0,1:T(8,128)S(1)}, f32[64,6,256]{2,0,1:T(8,128)}, u32[]{:S(2)}) copy-start(f32[64,6,256]{2,0,1:T(8,128)} %copy-done.13) | copy-start | bytes 1179652
  14.4 46.8 %collective-permute-start.4 = (f32[2,32,512]{2,1,0:T(8,128)}, f32[2,32,512]{2,1,0:T(8,128)}, u32[]{:S(2)}, u32[]{:S(2)}) collective-permute-start(f32[2,32,512]{2,1,0:T(8,128)} %get-tuple-element.68), channel_id=1, source_target_pairs={{0,32},{32,64},{64,96},{96,128},{128,160},{160,192},{192,224},{224... | collective-permute-start | bytes 393224 | tf_op jit(solution)/shard_map/ppermute | solution.py:17
  20.4 44.1 %collective-permute-start.5 = (f32[2,32,512]{2,1,0:T(8,128)}, f32[2,32,512]{2,1,0:T(8,128)}, u32[]{:S(2)}, u32[]{:S(2)}) collective-permute-start(f32[2,32,512]{2,1,0:T(8,128)} %get-tuple-element.67), channel_id=1, source_target_pairs={{32,0},{64,32},{96,64},{128,96},{160,128},{192,160},{224,192},{256... | collective-permute-start | bytes 393224 | tf_op jit(solution)/shard_map/ppermute | solution.py:19
  26.6 13.8 %collective-permute-start = (bf16[2,32,512]{2,1,0:T(8,128)(2,1)}, bf16[2,32,512]{2,1,0:T(8,128)(2,1)}, u32[]{:S(2)}, u32[]{:S(2)}) collective-permute-start(bf16[2,32,512]{2,1,0:T(8,128)(2,1)} %get-tuple-element.71), channel_id=1, source_target_pairs={{0,32},{32,64},{64,96},{96,128},{128,160},{160,192},{192,224},{224... | collective-permute-start | bytes 196616 | tf_op jit(solution)/shard_map/ppermute | solution.py:17
  29.0 11.4 %collective-permute-start.1 = (bf16[2,32,512]{2,1,0:T(8,128)(2,1)}, bf16[2,32,512]{2,1,0:T(8,128)(2,1)}, u32[]{:S(2)}, u32[]{:S(2)}) collective-permute-start(bf16[2,32,512]{2,1,0:T(8,128)(2,1)} %get-tuple-element.72), channel_id=1, source_target_pairs={{32,0},{64,32},{96,64},{128,96},{160,128},{192,160},{224,192},{256... | collective-permute-start | bytes 196616 | tf_op jit(solution)/shard_map/ppermute | solution.py:19
  37.7 2.7 copy-start.18
  45.7 17.1 %copy-start.8 = (f32[64,6,256]{2,0,1:T(8,128)S(1)}, f32[64,6,256]{2,0,1:T(8,128)}, u32[]{:S(2)}) copy-start(f32[64,6,256]{2,0,1:T(8,128)} %copy-done.7) | copy-start | bytes 1179652
  45.7 17.1 %copy-start.10 = (f32[64,6,256]{2,0,1:T(8,128)S(1)}, f32[64,6,256]{2,0,1:T(8,128)}, u32[]{:S(2)}) copy-start(f32[64,6,256]{2,0,1:T(8,128)} %copy-done.9) | copy-start | bytes 1179652
  51.8 23.2 %collective-permute-start.2 = (bf16[2,32,512]{2,1,0:T(8,128)(2,1)}, bf16[2,32,512]{2,1,0:T(8,128)(2,1)}, u32[]{:S(2)}, u32[]{:S(2)}) collective-permute-start(bf16[2,32,512]{2,1,0:T(8,128)(2,1)} %get-tuple-element.69), channel_id=1, source_target_pairs={{0,32},{32,64},{64,96},{96,128},{128,160},{160,192},{192,224},{224... | collective-permute-start | bytes 196616 | tf_op jit(solution)/shard_map/ppermute | solution.py:17
  53.7 21.3 %collective-permute-start.3 = (bf16[2,32,512]{2,1,0:T(8,128)(2,1)}, bf16[2,32,512]{2,1,0:T(8,128)(2,1)}, u32[]{:S(2)}, u32[]{:S(2)}) collective-permute-start(bf16[2,32,512]{2,1,0:T(8,128)(2,1)} %get-tuple-element.70), channel_id=1, source_target_pairs={{32,0},{64,32},{96,64},{128,96},{160,128},{192,160},{224,192},{256... | collective-permute-start | bytes 196616 | tf_op jit(solution)/shard_map/ppermute | solution.py:19
  73.0 1.3 copy-start.1
  73.0 1.3 copy-start.3
  73.0 1.2 copy-start.5
  73.1 1.2 copy-start.6
  74.3 1.0 copy-start.17
  80.6 1.1 copy-start.19
  81.7 3.1 %copy-start.22 = (bf16[1,2,32,1536]{3,2,1,0:T(8,128)(2,1)S(1)}, bf16[1,2,32,1536]{3,2,1,0:T(8,128)(2,1)}, u32[]{:S(2)}) copy-start(bf16[1,2,32,1536]{3,2,1,0:T(8,128)(2,1)} %convert_element_type.72) | copy-start | bytes 589828
  81.7 3.1 %copy-start.23 = (bf16[3,32,32]{2,1,0:T(8,128)(2,1)S(1)}, bf16[3,32,32]{2,1,0:T(8,128)(2,1)}, u32[]{:S(2)}) copy-start(bf16[3,32,32]{2,1,0:T(8,128)(2,1)} %param.17) | copy-start | bytes 18436
  82.8 3.0 copy-start.20
  82.8 3.0 copy-start.21
  86.7 206.6 %copy-start.2 = (f32[64,6,1,256]{3,0,1,2:T(8,128)S(1)}, f32[64,6,1,256]{3,0,1,2:T(8,128)}, u32[]{:S(2)}) copy-start(f32[64,6,1,256]{3,0,1,2:T(8,128)} %copy-done.1) | copy-start | bytes 1179652
  86.7 206.6 %copy-start.4 = (f32[64,6,1,256]{3,0,1,2:T(8,128)S(1)}, f32[64,6,1,256]{3,0,1,2:T(8,128)}, u32[]{:S(2)}) copy-start(f32[64,6,1,256]{3,0,1,2:T(8,128)} %copy-done.3) | copy-start | bytes 1179652
  90.2 201.4 %collective-permute-start.6 = (f32[2,32,512]{2,1,0:T(8,128)}, f32[2,32,512]{2,1,0:T(8,128)}, u32[]{:S(2)}, u32[]{:S(2)}) collective-permute-start(f32[2,32,512]{2,1,0:T(8,128)} %get-tuple-element.66), channel_id=1, source_target_pairs={{0,32},{32,64},{64,96},{96,128},{128,160},{160,192},{192,224},{224... | collective-permute-start | bytes 393224 | tf_op jit(solution)/shard_map/ppermute | solution.py:17
  93.9 201.0 %collective-permute-start.7 = (f32[2,32,512]{2,1,0:T(8,128)}, f32[2,32,512]{2,1,0:T(8,128)}, u32[]{:S(2)}, u32[]{:S(2)}) collective-permute-start(f32[2,32,512]{2,1,0:T(8,128)} %get-tuple-element.65), channel_id=1, source_target_pairs={{32,0},{64,32},{96,64},{128,96},{160,128},{192,160},{224,192},{256... | collective-permute-start | bytes 393224 | tf_op jit(solution)/shard_map/ppermute | solution.py:19
  294.9 7.3 %copy-start.16 = (f32[3,2,32,1536]{3,2,0,1:T(8,128)S(1)}, f32[3,2,32,1536]{3,2,0,1:T(8,128)}, u32[]{:S(2)}) copy-start(f32[3,2,32,1536]{3,2,0,1:T(8,128)} %copy-done.15) | copy-start | bytes 3538948
